TPU v7x, 128 devices: a whole 4x4x4 slice. The times are simulated.
128 devices in a mesh: dp: 16 (over x, z), fsdp: 8 (over y, core).
Axes of the slice: x: 4, y: 4, z: 4, core: 2. Of those that a mesh axis runs over, the one named last changes fastest.
Arguments:
- tokens: bfloat16 [2048, 4096], P('dp', 'fsdp'), may hold values from -6 to 6
- expert_ids: int32 [2048, 2], P('dp'), may hold values from 0 to 7, all different within a row; in each aligned block of 128 rows (0 to 127, 128 to 255, ...) at most 40 rows name the same one
- route_probs: float32 [2048, 2], P('dp'), may hold values from 0.1 to 0.9
- w_gate: bfloat16 [4096, 65536], P(None, ('dp', 'fsdp')), may hold values from -0.09375 to 0.09375
- w_up: bfloat16 [4096, 65536], P(None, ('dp', 'fsdp')), may hold values from -0.09375 to 0.09375
- w_down: bfloat16 [65536, 4096], P(('dp', 'fsdp')), may hold values from -0.0625 to 0.0625
- out_grad: bfloat16 [2048, 4096], P('dp', 'fsdp'), may hold values from -0.59765625 to 0.59765625
Outputs:
- mixed: bfloat16 [2048, 4096], P('dp', 'fsdp')
- token_grad: bfloat16 [2048, 4096], P('dp', 'fsdp')
- prob_grad: float32 [2048, 2], P('dp')
- gate_weight_grad: bfloat16 [4096, 65536], P(None, ('dp', 'fsdp'))
- up_weight_grad: bfloat16 [4096, 65536], P(None, ('dp', 'fsdp'))
- down_weight_grad: bfloat16 [65536, 4096], P(('dp', 'fsdp'))
Inputs may be any that keep to these rules, and one draw needn't show every extreme that they name: `expert_ids`: each token names two different experts. Within the 128 tokens of one dp index (aligned blocks of rows) no expert is named more than 40 times, and in some block one expert is named exactly 40 times.
All inputs are finite; a program needn't handle non-finite values.
Results may differ from a plain program's by a relative error of at most 0.019.
Values may be sent and summed in bfloat16 or wider, within the bound.
No kernel may reach another device: no remote copies, remote signals or barrier semaphores. Data moves between devices by JAX's collectives and lax.ppermute only.
A program may use at most 128 MiB of HBM per device.

v0:
```python
import jax
import jax.numpy as jnp
from jax import lax
from jax.sharding import PartitionSpec as P

E = 8
CAP = 40


def local(tokens, expert_ids, route_probs, w_gate, w_up, w_down, out_grad):
    dp_count = lax.axis_size("dp")
    groups = dp_count // E
    token_count = tokens.shape[0]
    slot_total = E * CAP
    routing = expert_ids.reshape(-1)
    onehot = (routing[:, None] == jnp.arange(E, dtype=jnp.int32)[None, :]).astype(jnp.int32)
    position = jnp.sum((jnp.cumsum(onehot, axis=0) - onehot) * onehot, axis=1)
    slot_of = (routing * CAP + position).reshape(token_count, 2)
    slot_index = jnp.arange(slot_total, dtype=jnp.int32)
    select_first = slot_of[:, 0:1] == slot_index[None, :]
    select_second = slot_of[:, 1:2] == slot_index[None, :]
    picker = jnp.logical_or(select_first, select_second)
    picker_bf = picker.astype(jnp.bfloat16)
    weighted = jnp.where(select_first, route_probs[:, 0:1], 0.0) + jnp.where(
        select_second, route_probs[:, 1:2], 0.0
    )
    contract_rows = (((0,), (0,)), ((), ()))
    back_dims = (((1,), (1,)), ((), ()))

    def place_rows(source, scaled):
        if scaled:
            placed = lax.dot_general(
                weighted,
                source.astype(jnp.float32),
                contract_rows,
                precision=lax.Precision.HIGHEST,
                preferred_element_type=jnp.float32,
            )
        else:
            placed = lax.dot_general(
                picker_bf, source, contract_rows, preferred_element_type=jnp.float32
            )
        placed = placed.astype(jnp.bfloat16).reshape(E, CAP, source.shape[1])
        return jnp.repeat(placed, groups, axis=0)

    def to_expert_layout(source, scaled):
        joined = lax.all_gather(source, "fsdp", axis=1, tiled=True)
        arrived = lax.all_to_all(
            place_rows(joined, scaled), "dp", split_axis=0, concat_axis=0, tiled=True
        )
        return arrived.reshape(dp_count * CAP, arrived.shape[2])

    def to_token_layout(partial_value):
        shares = lax.psum_scatter(
            partial_value.astype(jnp.bfloat16), "fsdp", scatter_dimension=1, tiled=True
        ).astype(jnp.float32)
        returned = lax.all_to_all(
            shares.reshape(dp_count, CAP, shares.shape[1]).astype(jnp.bfloat16),
            "dp",
            split_axis=0,
            concat_axis=0,
            tiled=True,
        ).astype(jnp.float32)
        return jnp.sum(returned.reshape(E, groups, CAP, returned.shape[2]), axis=1).reshape(
            slot_total, returned.shape[2]
        )

    expert_rows = to_expert_layout(tokens, False)
    gate_proj = jnp.dot(expert_rows, w_gate, preferred_element_type=jnp.float32)
    up_proj = jnp.dot(expert_rows, w_up, preferred_element_type=jnp.float32)
    sigmoid_gate = jax.nn.sigmoid(gate_proj)
    activated = gate_proj * sigmoid_gate
    hidden = (activated * up_proj).astype(jnp.bfloat16)
    out_partial = jnp.dot(hidden, w_down, preferred_element_type=jnp.float32)
    out_slots = to_token_layout(out_partial)
    first_pair = jnp.dot(
        select_first.astype(jnp.float32),
        out_slots,
        precision=lax.Precision.HIGHEST,
        preferred_element_type=jnp.float32,
    )
    second_pair = jnp.dot(
        select_second.astype(jnp.float32),
        out_slots,
        precision=lax.Precision.HIGHEST,
        preferred_element_type=jnp.float32,
    )
    mixed = (route_probs[:, 0:1] * first_pair + route_probs[:, 1:2] * second_pair).astype(
        jnp.bfloat16
    )
    grad_local = out_grad.astype(jnp.float32)
    prob_terms = jnp.stack(
        [jnp.sum(first_pair * grad_local, axis=1), jnp.sum(second_pair * grad_local, axis=1)],
        axis=1,
    )
    prob_grad = lax.psum(prob_terms, "fsdp")
    grad_rows = to_expert_layout(out_grad, True)
    hidden_grad = lax.dot_general(grad_rows, w_down, back_dims, preferred_element_type=jnp.float32)
    gate_grad = (
        hidden_grad * up_proj * sigmoid_gate * (1.0 + gate_proj * (1.0 - sigmoid_gate))
    ).astype(jnp.bfloat16)
    up_grad = (hidden_grad * activated).astype(jnp.bfloat16)
    gate_weight_grad = lax.dot_general(
        expert_rows, gate_grad, contract_rows, preferred_element_type=jnp.float32
    ).astype(jnp.bfloat16)
    up_weight_grad = lax.dot_general(
        expert_rows, up_grad, contract_rows, preferred_element_type=jnp.float32
    ).astype(jnp.bfloat16)
    down_weight_grad = lax.dot_general(
        hidden, grad_rows, contract_rows, preferred_element_type=jnp.float32
    ).astype(jnp.bfloat16)
    input_partial = lax.dot_general(
        gate_grad, w_gate, back_dims, preferred_element_type=jnp.float32
    )
    input_partial = input_partial + lax.dot_general(
        up_grad, w_up, back_dims, preferred_element_type=jnp.float32
    )
    input_slots = to_token_layout(input_partial)
    token_grad = jnp.dot(
        picker.astype(jnp.float32),
        input_slots,
        precision=lax.Precision.HIGHEST,
        preferred_element_type=jnp.float32,
    ).astype(jnp.bfloat16)
    return (mixed, token_grad, prob_grad, gate_weight_grad, up_weight_grad, down_weight_grad)


def solution(mesh):
    placed = (
        P("dp", "fsdp"),
        P("dp", None),
        P("dp", None),
        P(None, ("dp", "fsdp")),
        P(None, ("dp", "fsdp")),
        P(("dp", "fsdp"), None),
        P("dp", "fsdp"),
    )
    return jax.shard_map(
        local,
        mesh=mesh,
        in_specs=placed,
        out_specs=(
            P("dp", "fsdp"),
            P("dp", "fsdp"),
            P("dp", None),
            P(None, ("dp", "fsdp")),
            P(None, ("dp", "fsdp")),
            P(("dp", "fsdp"), None),
        ),
        check_vma=False,
    )
```

profile of v0, /device:TPU:2, one launch (start us, length us, event | category | flops | bytes accessed | tf_op | source)
XLA Modules:
  0.0 347.4 jit_solution(6366988755404527250)
XLA Ops:
  7.2 0.0 all-gather.3.cloned.1.call-start
  7.2 0.7 all-gather.3.cloned.1.call-update
  7.9 0.8 copy.21
  8.7 0.1 eq.59
  8.8 0.1 eq.55
  9.0 0.6 reduce-window.6
  9.6 0.2 slice_reduce_fusion
  9.8 0.1 fusion.23
  9.9 0.1 reduce_sum.48
  10.1 0.1 copy.23
  10.1 0.7 multiply_add_fusion
  10.8 24.6 %all-gather.3.cloned.1.call-done = bf16[128,4096]{1,0:T(8,128)(2,1)} async-done(((bf16[128,512]{1,0:T(8,128)(2,1)}), bf16[128,4096]{1,0:T(8,128)(2,1)}) %all-gather.3.cloned.1.call-update) | async-done | bytes 1048592 | tf_op jit(solution)/shard_map/all_gather | solution.py:47
  35.5 2.2 convolution_convert_fusion.5
  37.6 3.0 broadcast_in_dim.27
  40.6 7.5 %all-to-all-start = ((bf16[16,40,4096]{2,1,0:T(8,128)(2,1)}), bf16[16,40,4096]{2,1,0:T(8,128)(2,1)}, u32[]{:S(2)}, u32[]{:S(2)}) async-start(bf16[16,40,4096]{2,1,0:T(8,128)(2,1)} %bitcast.57), calls=%async_computation | async-start | bytes 10485760 | tf_op jit(solution)/shard_map/all_to_all | solution.py:48
  48.2 0.0 all-gather.5.cloned.1.call-start
  48.2 0.7 all-gather.5.cloned.1.call-update
  49.0 24.8 %all-gather.5.cloned.1.call-done = bf16[128,4096]{1,0:T(8,128)(2,1)} async-done(((bf16[128,512]{1,0:T(8,128)(2,1)}), bf16[128,4096]{1,0:T(8,128)(2,1)}) %all-gather.5.cloned.1.call-update) | async-done | bytes 1048592 | tf_op jit(solution)/shard_map/all_gather | solution.py:47
  73.8 3.6 %convolution_convert_fusion.4 = bf16[320,4096]{1,0:T(8,128)(2,1)S(1)} fusion(bf16[128,4096]{1,0:T(8,128)(2,1)} %all-gather.5.cloned.1.call-done, f32[128]{0:T(128)S(1)} %get-tuple-element.13, f32[128]{0:T(128)S(1)} %get-tuple-element.12, s32[128]{0:T(128)S(1)} %get-tuple-element.15, s32[128]{0:T(128)S(1)} %get-tuple-element.14), kind=kOutput, calls=%fused_computation.5 | convolution fusion | flops 2014781440 | bytes 3672064 | tf_op jit(solution)/shard_map/dot_general | solution.py:32
  77.4 38.4 %all-to-all-done = bf16[16,40,4096]{2,1,0:T(8,128)(2,1)} async-done(((bf16[16,40,4096]{2,1,0:T(8,128)(2,1)}), bf16[16,40,4096]{2,1,0:T(8,128)(2,1)}, u32[]{:S(2)}, u32[]{:S(2)}) %all-to-all-start) | async-done | bytes 5242912 | tf_op jit(solution)/shard_map/all_to_all | solution.py:48
  115.7 3.0 broadcast_in_dim.31
  118.7 24.0 %all-to-all-start.2 = ((bf16[16,40,4096]{2,1,0:T(8,128)(2,1)}), bf16[16,40,4096]{2,1,0:T(8,128)(2,1)}, u32[]{:S(2)}, u32[]{:S(2)}) async-start(bf16[16,40,4096]{2,1,0:T(8,128)(2,1)} %bitcast.58), calls=%async_computation.3 | async-start | bytes 10485760 | tf_op jit(solution)/shard_map/all_to_all | solution.py:48
  142.7 0.2 reduce-scatter.3.cloned.1.call-start
  142.9 0.0 copy-start.3
  143.0 7.8 %fusion.26 = f32[640,512]{1,0:T(8,128)} fusion(bf16[640,4096]{1,0:T(8,128)(2,1)} %bitcast.7, bf16[4096,512]{1,0:T(8,128)(2,1)} %param.10), kind=kOutput, calls=%fused_computation.53 | convolution fusion | flops 2684354560 | bytes 10747904 | tf_op jit(solution)/shard_map/dot_general | solution.py:69
  150.8 6.4 %fusion.27 = f32[640,512]{1,0:T(8,128)} fusion(bf16[640,4096]{1,0:T(8,128)(2,1)} %bitcast.7, bf16[4096,512]{1,0:T(8,128)(2,1)S(1)} %copy-done.3), kind=kOutput, calls=%fused_computation.54 | convolution fusion | flops 2684354560 | bytes 10747904 | tf_op jit(solution)/shard_map/dot_general | solution.py:70
  157.2 53.1 %all-to-all-done.2 = bf16[16,40,4096]{2,1,0:T(8,128)(2,1)} async-done(((bf16[16,40,4096]{2,1,0:T(8,128)(2,1)}), bf16[16,40,4096]{2,1,0:T(8,128)(2,1)}, u32[]{:S(2)}, u32[]{:S(2)}) %all-to-all-start.2) | async-done | bytes 5242912 | tf_op jit(solution)/shard_map/all_to_all | solution.py:48
  210.3 8.0 %multiply_convert_fusion = (bf16[640,512]{1,0:T(8,128)(2,1)S(1)}, bf16[640,512]{1,0:T(8,128)(2,1)S(1)}, bf16[640,512]{1,0:T(8,128)(2,1)S(1)}) fusion(f32[640,512]{1,0:T(8,128)} %fusion.26, f32[640,512]{1,0:T(8,128)} %fusion.27, bf16[640,4096]{1,0:T(8,128)(2,1)} %bitcast.14, bf16[512,4096]{1,0:T(8,128)(2,1)} %param.12), kind=kOutput, calls=%fused_computation.9 | convolution fusion | flops 2689269760 | bytes 14024704 | tf_op jit(solution)/shard_map/dot_general | solution.py:98
  218.3 4.7 %convolution_convert_fusion = bf16[640,4096]{1,0:T(8,128)(2,1)} fusion(bf16[640,512]{1,0:T(8,128)(2,1)S(1)} %get-tuple-element.10, bf16[512,4096]{1,0:T(8,128)(2,1)S(1)} %copy-done.2), kind=kOutput, calls=%fused_computation.1 | convolution fusion | flops 2686976000 | bytes 10092544 | tf_op jit(solution)/shard_map/dot_general | solution.py:74
  223.0 0.0 reduce-scatter.3.cloned.1.call-update
  223.0 0.3 reduce-scatter.5.cloned.1.call-start
  223.3 0.0 copy-start.4
  223.3 4.9 %fusion.28 = f32[640,4096]{1,0:T(8,128)S(1)} fusion(bf16[640,512]{1,0:T(8,128)(2,1)S(1)} %get-tuple-element.9, bf16[4096,512]{1,0:T(8,128)(2,1)} %param.10), kind=kOutput, calls=%fused_computation.55 | convolution fusion | flops 2684354560 | bytes 15335424 | tf_op jit(solution)/shard_map/dot_general | solution.py:112
  228.2 4.8 %add_convert_fusion = bf16[640,4096]{1,0:T(8,128)(2,1)} fusion(f32[640,4096]{1,0:T(8,128)S(1)} %fusion.28, bf16[640,512]{1,0:T(8,128)(2,1)S(1)} %get-tuple-element.8, bf16[4096,512]{1,0:T(8,128)(2,1)S(1)} %copy-done.4), kind=kOutput, calls=%fused_computation | convolution fusion | flops 2689597440 | bytes 20578304 | tf_op jit(solution)/shard_map/dot_general | solution.py:115
  232.9 0.0 reduce-scatter.5.cloned.1.call-update
  233.0 7.5 %convolution_convert_fusion.1 = bf16[512,4096]{1,0:T(8,128)(2,1)} fusion(bf16[640,512]{1,0:T(8,128)(2,1)S(1)} %get-tuple-element.10, bf16[640,4096]{1,0:T(8,128)(2,1)} %bitcast.14), kind=kOutput, calls=%fused_computation.2 | convolution fusion | flops 2686451712 | bytes 10092544 | tf_op jit(solution)/shard_map/dot_general | solution.py:109
  240.5 7.5 %convolution_convert_fusion.2 = bf16[4096,512]{1,0:T(8,128)(2,1)} fusion(bf16[640,4096]{1,0:T(8,128)(2,1)} %bitcast.7, bf16[640,512]{1,0:T(8,128)(2,1)S(1)} %get-tuple-element.8), kind=kOutput, calls=%fused_computation.3 | convolution fusion | flops 2686451712 | bytes 10092544 | tf_op jit(solution)/shard_map/dot_general | solution.py:106
  248.0 26.8 %reduce-scatter.3.cloned.1.call-done = bf16[640,512]{1,0:T(8,128)(2,1)} async-done(((bf16[640,4096]{1,0:T(8,128)(2,1)}), bf16[640,512]{1,0:T(8,128)(2,1)}) %reduce-scatter.3.cloned.1.call-update) | async-done | bytes 655376 | tf_op jit(solution)/shard_map/reduce_scatter | solution.py:54
  274.8 7.5 %all-to-all-start.1 = ((bf16[16,40,512]{2,1,0:T(8,128)(2,1)}), bf16[16,40,512]{2,1,0:T(8,128)(2,1)S(1)}, u32[]{:S(2)}, u32[]{:S(2)}) async-start(bf16[16,40,512]{2,1,0:T(8,128)(2,1)} %bitcast.65), calls=%async_computation.2 | async-start | bytes 1310720 | tf_op jit(solution)/shard_map/all_to_all | solution.py:57
  282.3 7.6 %convolution_convert_fusion.3 = bf16[4096,512]{1,0:T(8,128)(2,1)} fusion(bf16[640,4096]{1,0:T(8,128)(2,1)} %bitcast.7, bf16[640,512]{1,0:T(8,128)(2,1)S(1)} %get-tuple-element.9), kind=kOutput, calls=%fused_computation.4 | convolution fusion | flops 2686451712 | bytes 10092544 | tf_op jit(solution)/shard_map/dot_general | solution.py:103
  289.9 26.6 %reduce-scatter.5.cloned.1.call-done = bf16[640,512]{1,0:T(8,128)(2,1)} async-done(((bf16[640,4096]{1,0:T(8,128)(2,1)}), bf16[640,512]{1,0:T(8,128)(2,1)}) %reduce-scatter.5.cloned.1.call-update) | async-done | bytes 655376 | tf_op jit(solution)/shard_map/reduce_scatter | solution.py:54
  316.5 7.5 %all-to-all-start.3 = ((bf16[16,40,512]{2,1,0:T(8,128)(2,1)}), bf16[16,40,512]{2,1,0:T(8,128)(2,1)S(1)}, u32[]{:S(2)}, u32[]{:S(2)}) async-start(bf16[16,40,512]{2,1,0:T(8,128)(2,1)} %bitcast.64), calls=%async_computation.5 | async-start | bytes 1310720 | tf_op jit(solution)/shard_map/all_to_all | solution.py:57
  324.0 0.1 convert_reduce_fusion.1
  324.1 0.5 fusion.6
  324.6 1.1 fusion.1
  325.7 13.9 %psum.7 = f32[128,2]{0,1:T(2,128)} all-reduce(f32[128,2]{0,1:T(2,128)S(1)} %pad_maximum_fusion), channel_id=1, replica_groups=mesh['dp'=16,'fsdp'=8] {'fsdp'}, use_global_device_ids=true, to_apply=%region_9.10 | all-reduce | flops 256 | bytes 2048 | tf_op jit(solution)/shard_map/psum | solution.py:96
  339.6 0.1 convert_reduce_fusion
  339.7 1.1 convolution_convert_fusion.6
  (16 shorter events, 0.1 us)
Async XLA Ops:
  7.2 28.3 %all-gather.3.cloned.1.call-start = ((), (), s32[]{:S(2)}) async-start(), calls=%async_computation.6 | async-start | bytes 1179648 | tf_op jit(solution)/shard_map/all_gather | solution.py:47
  40.6 8.3 %copy-start.1 = (f32[128,2]{0,1:T(2,128)S(1)}, f32[128,2]{0,1:T(2,128)}, u32[]{:S(2)}) copy-start(f32[128,2]{0,1:T(2,128)} %param.9) | copy-start | bytes 3076
  40.6 75.1 %all-to-all-start = ((bf16[16,40,4096]{2,1,0:T(8,128)(2,1)}), bf16[16,40,4096]{2,1,0:T(8,128)(2,1)}, u32[]{:S(2)}, u32[]{:S(2)}) async-start(bf16[16,40,4096]{2,1,0:T(8,128)(2,1)} %bitcast.57), calls=%async_computation | async-start | bytes 10485760 | tf_op jit(solution)/shard_map/all_to_all | solution.py:48
  48.2 25.6 %all-gather.5.cloned.1.call-start = ((), (), s32[]{:S(2)}) async-start(), calls=%async_computation.8 | async-start | bytes 1179648 | tf_op jit(solution)/shard_map/all_gather | solution.py:47
  118.7 91.6 %all-to-all-start.2 = ((bf16[16,40,4096]{2,1,0:T(8,128)(2,1)}), bf16[16,40,4096]{2,1,0:T(8,128)(2,1)}, u32[]{:S(2)}, u32[]{:S(2)}) async-start(bf16[16,40,4096]{2,1,0:T(8,128)(2,1)} %bitcast.58), calls=%async_computation.3 | async-start | bytes 10485760 | tf_op jit(solution)/shard_map/all_to_all | solution.py:48
  142.7 132.1 %reduce-scatter.3.cloned.1.call-start = ((), (), s32[]{:S(2)}) async-start(), calls=%async_computation.7 | async-start | bytes 5898240 | tf_op jit(solution)/shard_map/reduce_scatter | solution.py:54
  142.9 7.8 %copy-start.3 = (bf16[4096,512]{1,0:T(8,128)(2,1)S(1)}, bf16[4096,512]{1,0:T(8,128)(2,1)}, u32[]{:S(2)}) copy-start(bf16[4096,512]{1,0:T(8,128)(2,1)} %param.11) | copy-start | bytes 12582916
  210.3 8.0 %copy-start.2 = (bf16[512,4096]{1,0:T(8,128)(2,1)S(1)}, bf16[512,4096]{1,0:T(8,128)(2,1)}, u32[]{:S(2)}) copy-start(bf16[512,4096]{1,0:T(8,128)(2,1)} %param.12) | copy-start | bytes 12582916
  223.0 93.5 %reduce-scatter.5.cloned.1.call-start = ((), (), s32[]{:S(2)}) async-start(), calls=%async_computation.9 | async-start | bytes 5898240 | tf_op jit(solution)/shard_map/reduce_scatter | solution.py:54
  223.3 4.9 %copy-start.4 = (bf16[4096,512]{1,0:T(8,128)(2,1)S(1)}, bf16[4096,512]{1,0:T(8,128)(2,1)}, u32[]{:S(2)}) copy-start(bf16[4096,512]{1,0:T(8,128)(2,1)} %param.11) | copy-start | bytes 12582916
  274.8 41.7 %all-to-all-start.1 = ((bf16[16,40,512]{2,1,0:T(8,128)(2,1)}), bf16[16,40,512]{2,1,0:T(8,128)(2,1)S(1)}, u32[]{:S(2)}, u32[]{:S(2)}) async-start(bf16[16,40,512]{2,1,0:T(8,128)(2,1)} %bitcast.65), calls=%async_computation.2 | async-start | bytes 1310720 | tf_op jit(solution)/shard_map/all_to_all | solution.py:57
  282.2 42.3 %copy-start = (bf16[128,512]{1,0:T(8,128)(2,1)S(1)}, bf16[128,512]{1,0:T(8,128)(2,1)}, u32[]{:S(2)}) copy-start(bf16[128,512]{1,0:T(8,128)(2,1)} %param.13) | copy-start | bytes 393220
  316.5 23.1 %all-to-all-start.3 = ((bf16[16,40,512]{2,1,0:T(8,128)(2,1)}), bf16[16,40,512]{2,1,0:T(8,128)(2,1)S(1)}, u32[]{:S(2)}, u32[]{:S(2)}) async-start(bf16[16,40,512]{2,1,0:T(8,128)(2,1)} %bitcast.64), calls=%async_computation.5 | async-start | bytes 1310720 | tf_op jit(solution)/shard_map/all_to_all | solution.py:57
Sparse Core Ops, SparseCore 0:
  9.7 25.7 all-gather.2
  50.7 23.0 all-gather.4
  223.1 51.6 reduce-scatter.2
  277.0 39.3 reduce-scatter.4
where the time goes:
time: 348 us; the launch traced here: 347 us
  waiting for transfers between devices  196 us (56%)
  matrix products  67.6 us (19%)
  starting transfers between devices  47 us (14%)
  blocking collectives  13.9 us (4%)
  between operations  13.9 us (4%)
  local copies, waits for them, and re-layouts  7.52 us (2%)
    all_to_all x2, waiting for transfers between devices, to_expert_layout(): lax.all_to_all(place_rows(joined, scaled), 'dp', split_axis=0, concat_axi...  91.5 us
    reduce_scatter x2, waiting for transfers between devices, to_token_layout(): lax.psum_scatter(partial_value.astype(jnp.bfloat16), 'fsdp', scatter_dime...  53.4 us
    all_gather x2, waiting for transfers between devices, to_expert_layout(): joined = lax.all_gather(source, 'fsdp', axis=1, tiled=True)  49.5 us
    all_to_all x2, starting transfers between devices, to_expert_layout(): lax.all_to_all(place_rows(joined, scaled), 'dp', split_axis=0, concat_axi...  31.5 us
    all_to_all x2, starting transfers between devices, to_token_layout(): lax.all_to_all(shares.reshape(dp_count, CAP, shares.shape[1]).astype(jnp....  15 us
    psum x1, blocking collectives, local(): prob_grad = lax.psum(prob_terms, 'fsdp')  13.9 us
    dot_general x1, matrix products, local(): lax.dot_general(grad_rows, w_down, back_dims, preferred_element_type=jnp....  7.96 us
    dot_general x1, matrix products, local(): gate_proj = jnp.dot(expert_rows, w_gate, preferred_element_type=jnp.float32)  7.81 us
  transfers between devices with their start and end apart: 8, of which 6 were waited for; matrix products, arithmetic and copies ran while one was open for 16% of the time, Pallas kernels for 0%

commit v1 on v0

--- a/solution.py
+++ b/solution.py
@@ -1,3 +1,4 @@
+import functools
 import jax
 import jax.numpy as jnp
 from jax import lax
@@ -5,6 +6,14 @@
 
 E = 8
 CAP = 40
+
+
+def counts_create(sample, axis_name):
+    carry_out = lax.all_gather(sample, axis_name=axis_name)
+    return jnp.sum(carry_out, axis=0)
+
+
+process_chains_for = functools.partial(counts_create, axis_name="fsdp")
 
 
 def local(tokens, expert_ids, route_probs, w_gate, w_up, w_down, out_grad):
@@ -93,7 +102,7 @@
         [jnp.sum(first_pair * grad_local, axis=1), jnp.sum(second_pair * grad_local, axis=1)],
         axis=1,
     )
-    prob_grad = lax.psum(prob_terms, "fsdp")
+    prob_grad = process_chains_for(prob_terms)
     grad_rows = to_expert_layout(out_grad, True)
     hidden_grad = lax.dot_general(grad_rows, w_down, back_dims, preferred_element_type=jnp.float32)
     gate_grad = (

time: 348 us -> 343 us (0.986)
  blocking collectives: 13.9 us -> 7.84 us
    psum x1 -> x0, blocking collectives: 13.9 us -> none  [local(): prob_grad = lax.psum(prob_terms, 'fsdp')]
    all_gather x0 -> x1, blocking collectives: none -> 7.84 us  [counts_create(): carry_out = lax.all_gather(sample, axis_name=axis_name)]
where the time goes in v1:
time: 343 us; the launch traced here: 342 us
  waiting for transfers between devices  196 us (57%)
  matrix products  67.6 us (20%)
  starting transfers between devices  47 us (14%)
  between operations  13.9 us (4%)
  blocking collectives  7.84 us (2%)
  local copies, waits for them, and re-layouts  7.52 us (2%)
    all_to_all x2, waiting for transfers between devices, to_expert_layout(): lax.all_to_all(place_rows(joined, scaled), 'dp', split_axis=0, concat_axi...  91.5 us
    reduce_scatter x2, waiting for transfers between devices, to_token_layout(): lax.psum_scatter(partial_value.astype(jnp.bfloat16), 'fsdp', scatter_dime...  53.4 us
    all_gather x2, waiting for transfers between devices, to_expert_layout(): joined = lax.all_gather(source, 'fsdp', axis=1, tiled=True)  49.5 us
    all_to_all x2, starting transfers between devices, to_expert_layout(): lax.all_to_all(place_rows(joined, scaled), 'dp', split_axis=0, concat_axi...  31.5 us
    all_to_all x2, starting transfers between devices, to_token_layout(): lax.all_to_all(shares.reshape(dp_count, CAP, shares.shape[1]).astype(jnp....  15 us
    dot_general x1, matrix products, local(): lax.dot_general(grad_rows, w_down, back_dims, preferred_element_type=jnp....  7.96 us
    all_gather x1, blocking collectives, counts_create(): carry_out = lax.all_gather(sample, axis_name=axis_name)  7.84 us
    dot_general x1, matrix products, local(): gate_proj = jnp.dot(expert_rows, w_gate, preferred_element_type=jnp.float32)  7.81 us
  transfers between devices with their start and end apart: 8, of which 6 were waited for; matrix products, arithmetic and copies ran while one was open for 16% of the time, Pallas kernels for 0%

profile of v1, /device:TPU:2, one launch (start us, length us, event | category | flops | bytes accessed | tf_op | source)
XLA Modules:
  0.0 341.9 jit_solution(956578498228259277)
XLA Ops:
  7.2 0.0 all-gather.4.cloned.1.call-start
  7.2 0.7 all-gather.4.cloned.1.call-update
  7.9 0.8 copy.21
  8.7 0.1 eq.59
  8.8 0.1 eq.55
  9.0 0.6 reduce-window.6
  9.6 0.2 slice_reduce_fusion
  9.8 0.1 fusion.23
  9.9 0.1 reduce_sum.57
  10.1 0.1 copy.23
  10.1 0.7 multiply_add_fusion
  10.8 24.6 %all-gather.4.cloned.1.call-done = bf16[128,4096]{1,0:T(8,128)(2,1)} async-done(((bf16[128,512]{1,0:T(8,128)(2,1)}), bf16[128,4096]{1,0:T(8,128)(2,1)}) %all-gather.4.cloned.1.call-update) | async-done | bytes 1048592 | tf_op jit(solution)/shard_map/all_gather | solution.py:56
  35.5 2.2 convolution_convert_fusion.5
  37.6 3.0 broadcast_in_dim.27
  40.6 7.5 %all-to-all-start = ((bf16[16,40,4096]{2,1,0:T(8,128)(2,1)}), bf16[16,40,4096]{2,1,0:T(8,128)(2,1)}, u32[]{:S(2)}, u32[]{:S(2)}) async-start(bf16[16,40,4096]{2,1,0:T(8,128)(2,1)} %bitcast.62), calls=%async_computation | async-start | bytes 10485760 | tf_op jit(solution)/shard_map/all_to_all | solution.py:57
  48.2 0.0 all-gather.6.cloned.1.call-start
  48.2 0.7 all-gather.6.cloned.1.call-update
  49.0 24.8 %all-gather.6.cloned.1.call-done = bf16[128,4096]{1,0:T(8,128)(2,1)} async-done(((bf16[128,512]{1,0:T(8,128)(2,1)}), bf16[128,4096]{1,0:T(8,128)(2,1)}) %all-gather.6.cloned.1.call-update) | async-done | bytes 1048592 | tf_op jit(solution)/shard_map/all_gather | solution.py:56
  73.8 3.6 %convolution_convert_fusion.4 = bf16[320,4096]{1,0:T(8,128)(2,1)S(1)} fusion(bf16[128,4096]{1,0:T(8,128)(2,1)} %all-gather.6.cloned.1.call-done, f32[128]{0:T(128)S(1)} %get-tuple-element.13, f32[128]{0:T(128)S(1)} %get-tuple-element.12, s32[128]{0:T(128)S(1)} %get-tuple-element.15, s32[128]{0:T(128)S(1)} %get-tuple-element.14), kind=kOutput, calls=%fused_computation.5 | convolution fusion | flops 2014781440 | bytes 3672064 | tf_op jit(solution)/shard_map/dot_general | solution.py:41
  77.4 38.4 %all-to-all-done = bf16[16,40,4096]{2,1,0:T(8,128)(2,1)} async-done(((bf16[16,40,4096]{2,1,0:T(8,128)(2,1)}), bf16[16,40,4096]{2,1,0:T(8,128)(2,1)}, u32[]{:S(2)}, u32[]{:S(2)}) %all-to-all-start) | async-done | bytes 5242912 | tf_op jit(solution)/shard_map/all_to_all | solution.py:57
  115.7 3.0 broadcast_in_dim.31
  118.7 24.0 %all-to-all-start.2 = ((bf16[16,40,4096]{2,1,0:T(8,128)(2,1)}), bf16[16,40,4096]{2,1,0:T(8,128)(2,1)}, u32[]{:S(2)}, u32[]{:S(2)}) async-start(bf16[16,40,4096]{2,1,0:T(8,128)(2,1)} %bitcast.63), calls=%async_computation.3 | async-start | bytes 10485760 | tf_op jit(solution)/shard_map/all_to_all | solution.py:57
  142.7 0.2 reduce-scatter.3.cloned.1.call-start
  142.9 0.0 copy-start.3
  143.0 7.8 %fusion.26 = f32[640,512]{1,0:T(8,128)} fusion(bf16[640,4096]{1,0:T(8,128)(2,1)} %bitcast.7, bf16[4096,512]{1,0:T(8,128)(2,1)} %param.10), kind=kOutput, calls=%fused_computation.54 | convolution fusion | flops 2684354560 | bytes 10747904 | tf_op jit(solution)/shard_map/dot_general | solution.py:78
  150.8 6.4 %fusion.27 = f32[640,512]{1,0:T(8,128)} fusion(bf16[640,4096]{1,0:T(8,128)(2,1)} %bitcast.7, bf16[4096,512]{1,0:T(8,128)(2,1)S(1)} %copy-done.3), kind=kOutput, calls=%fused_computation.55 | convolution fusion | flops 2684354560 | bytes 10747904 | tf_op jit(solution)/shard_map/dot_general | solution.py:79
  157.2 53.1 %all-to-all-done.2 = bf16[16,40,4096]{2,1,0:T(8,128)(2,1)} async-done(((bf16[16,40,4096]{2,1,0:T(8,128)(2,1)}), bf16[16,40,4096]{2,1,0:T(8,128)(2,1)}, u32[]{:S(2)}, u32[]{:S(2)}) %all-to-all-start.2) | async-done | bytes 5242912 | tf_op jit(solution)/shard_map/all_to_all | solution.py:57
  210.3 8.0 %multiply_convert_fusion = (bf16[640,512]{1,0:T(8,128)(2,1)S(1)}, bf16[640,512]{1,0:T(8,128)(2,1)S(1)}, bf16[640,512]{1,0:T(8,128)(2,1)S(1)}) fusion(f32[640,512]{1,0:T(8,128)} %fusion.26, f32[640,512]{1,0:T(8,128)} %fusion.27, bf16[640,4096]{1,0:T(8,128)(2,1)} %bitcast.14, bf16[512,4096]{1,0:T(8,128)(2,1)} %param.12), kind=kOutput, calls=%fused_computation.9 | convolution fusion | flops 2689269760 | bytes 14024704 | tf_op jit(solution)/shard_map/dot_general | solution.py:107
  218.3 4.7 %convolution_convert_fusion = bf16[640,4096]{1,0:T(8,128)(2,1)} fusion(bf16[640,512]{1,0:T(8,128)(2,1)S(1)} %get-tuple-element.10, bf16[512,4096]{1,0:T(8,128)(2,1)S(1)} %copy-done.2), kind=kOutput, calls=%fused_computation.1 | convolution fusion | flops 2686976000 | bytes 10092544 | tf_op jit(solution)/shard_map/dot_general | solution.py:83
  223.0 0.0 reduce-scatter.3.cloned.1.call-update
  223.0 0.3 reduce-scatter.5.cloned.1.call-start
  223.3 4.9 %fusion.28 = f32[640,4096]{1,0:T(8,128)S(1)} fusion(bf16[640,512]{1,0:T(8,128)(2,1)S(1)} %get-tuple-element.9, bf16[4096,512]{1,0:T(8,128)(2,1)} %param.10), kind=kOutput, calls=%fused_computation.56 | convolution fusion | flops 2684354560 | bytes 15335424 | tf_op jit(solution)/shard_map/dot_general | solution.py:121
  228.2 4.8 %add_convert_fusion = bf16[640,4096]{1,0:T(8,128)(2,1)} fusion(f32[640,4096]{1,0:T(8,128)S(1)} %fusion.28, bf16[640,512]{1,0:T(8,128)(2,1)S(1)} %get-tuple-element.8, bf16[4096,512]{1,0:T(8,128)(2,1)S(1)} %copy-done.4), kind=kOutput, calls=%fused_computation | convolution fusion | flops 2689597440 | bytes 20578304 | tf_op jit(solution)/shard_map/dot_general | solution.py:124
  232.9 0.0 reduce-scatter.5.cloned.1.call-update
  233.0 7.5 %convolution_convert_fusion.1 = bf16[512,4096]{1,0:T(8,128)(2,1)} fusion(bf16[640,512]{1,0:T(8,128)(2,1)S(1)} %get-tuple-element.10, bf16[640,4096]{1,0:T(8,128)(2,1)} %bitcast.14), kind=kOutput, calls=%fused_computation.2 | convolution fusion | flops 2686451712 | bytes 10092544 | tf_op jit(solution)/shard_map/dot_general | solution.py:118
  240.5 7.5 %convolution_convert_fusion.2 = bf16[4096,512]{1,0:T(8,128)(2,1)} fusion(bf16[640,4096]{1,0:T(8,128)(2,1)} %bitcast.7, bf16[640,512]{1,0:T(8,128)(2,1)S(1)} %get-tuple-element.8), kind=kOutput, calls=%fused_computation.3 | convolution fusion | flops 2686451712 | bytes 10092544 | tf_op jit(solution)/shard_map/dot_general | solution.py:115
  248.0 26.8 %reduce-scatter.3.cloned.1.call-done = bf16[640,512]{1,0:T(8,128)(2,1)} async-done(((bf16[640,4096]{1,0:T(8,128)(2,1)}), bf16[640,512]{1,0:T(8,128)(2,1)}) %reduce-scatter.3.cloned.1.call-update) | async-done | bytes 655376 | tf_op jit(solution)/shard_map/reduce_scatter | solution.py:63
  274.8 7.5 %all-to-all-start.1 = ((bf16[16,40,512]{2,1,0:T(8,128)(2,1)}), bf16[16,40,512]{2,1,0:T(8,128)(2,1)S(1)}, u32[]{:S(2)}, u32[]{:S(2)}) async-start(bf16[16,40,512]{2,1,0:T(8,128)(2,1)} %bitcast.70), calls=%async_computation.2 | async-start | bytes 1310720 | tf_op jit(solution)/shard_map/all_to_all | solution.py:66
  282.3 7.6 %convolution_convert_fusion.3 = bf16[4096,512]{1,0:T(8,128)(2,1)} fusion(bf16[640,4096]{1,0:T(8,128)(2,1)} %bitcast.7, bf16[640,512]{1,0:T(8,128)(2,1)S(1)} %get-tuple-element.9), kind=kOutput, calls=%fused_computation.4 | convolution fusion | flops 2686451712 | bytes 10092544 | tf_op jit(solution)/shard_map/dot_general | solution.py:112
  289.9 26.6 %reduce-scatter.5.cloned.1.call-done = bf16[640,512]{1,0:T(8,128)(2,1)} async-done(((bf16[640,4096]{1,0:T(8,128)(2,1)}), bf16[640,512]{1,0:T(8,128)(2,1)}) %reduce-scatter.5.cloned.1.call-update) | async-done | bytes 655376 | tf_op jit(solution)/shard_map/reduce_scatter | solution.py:63
  316.5 7.5 %all-to-all-start.3 = ((bf16[16,40,512]{2,1,0:T(8,128)(2,1)}), bf16[16,40,512]{2,1,0:T(8,128)(2,1)S(1)}, u32[]{:S(2)}, u32[]{:S(2)}) async-start(bf16[16,40,512]{2,1,0:T(8,128)(2,1)} %bitcast.69), calls=%async_computation.5 | async-start | bytes 1310720 | tf_op jit(solution)/shard_map/all_to_all | solution.py:66
  324.0 0.1 convert_reduce_fusion.1
  324.1 0.5 fusion.6
  324.6 1.1 fusion.1
  325.7 7.8 %all-gather = f32[1024,2]{0,1:T(2,128)S(1)} all-gather(f32[128,2]{0,1:T(2,128)S(1)} %pad_maximum_fusion), channel_id=2, replica_groups=mesh['dp'=16,'fsdp'=8] {'fsdp'}, dimensions={0}, use_global_device_ids=true | all-gather | bytes 9216 | tf_op jit(solution)/shard_map/all_gather | solution.py:12
  333.5 0.6 bitcast_reduce_fusion
  334.1 0.1 convert_reduce_fusion
  334.2 1.1 convolution_convert_fusion.6
  (17 shorter events, 0.1 us)
Async XLA Ops:
  7.2 28.3 %all-gather.4.cloned.1.call-start = ((), (), s32[]{:S(2)}) async-start(), calls=%async_computation.6 | async-start | bytes 1179648 | tf_op jit(solution)/shard_map/all_gather | solution.py:56
  40.6 8.3 %copy-start.1 = (f32[128,2]{0,1:T(2,128)S(1)}, f32[128,2]{0,1:T(2,128)}, u32[]{:S(2)}) copy-start(f32[128,2]{0,1:T(2,128)} %param.9) | copy-start | bytes 3076
  40.6 75.1 %all-to-all-start = ((bf16[16,40,4096]{2,1,0:T(8,128)(2,1)}), bf16[16,40,4096]{2,1,0:T(8,128)(2,1)}, u32[]{:S(2)}, u32[]{:S(2)}) async-start(bf16[16,40,4096]{2,1,0:T(8,128)(2,1)} %bitcast.62), calls=%async_computation | async-start | bytes 10485760 | tf_op jit(solution)/shard_map/all_to_all | solution.py:57
  48.2 25.6 %all-gather.6.cloned.1.call-start = ((), (), s32[]{:S(2)}) async-start(), calls=%async_computation.8 | async-start | bytes 1179648 | tf_op jit(solution)/shard_map/all_gather | solution.py:56
  118.7 91.6 %all-to-all-start.2 = ((bf16[16,40,4096]{2,1,0:T(8,128)(2,1)}), bf16[16,40,4096]{2,1,0:T(8,128)(2,1)}, u32[]{:S(2)}, u32[]{:S(2)}) async-start(bf16[16,40,4096]{2,1,0:T(8,128)(2,1)} %bitcast.63), calls=%async_computation.3 | async-start | bytes 10485760 | tf_op jit(solution)/shard_map/all_to_all | solution.py:57
  142.7 132.1 %reduce-scatter.3.cloned.1.call-start = ((), (), s32[]{:S(2)}) async-start(), calls=%async_computation.7 | async-start | bytes 5898240 | tf_op jit(solution)/shard_map/reduce_scatter | solution.py:63
  142.9 7.8 %copy-start.3 = (bf16[4096,512]{1,0:T(8,128)(2,1)S(1)}, bf16[4096,512]{1,0:T(8,128)(2,1)}, u32[]{:S(2)}) copy-start(bf16[4096,512]{1,0:T(8,128)(2,1)} %param.11) | copy-start | bytes 12582916
  210.3 8.0 %copy-start.2 = (bf16[512,4096]{1,0:T(8,128)(2,1)S(1)}, bf16[512,4096]{1,0:T(8,128)(2,1)}, u32[]{:S(2)}) copy-start(bf16[512,4096]{1,0:T(8,128)(2,1)} %param.12) | copy-start | bytes 12582916
  223.0 93.5 %reduce-scatter.5.cloned.1.call-start = ((), (), s32[]{:S(2)}) async-start(), calls=%async_computation.9 | async-start | bytes 5898240 | tf_op jit(solution)/shard_map/reduce_scatter | solution.py:63
  223.3 4.9 %copy-start.4 = (bf16[4096,512]{1,0:T(8,128)(2,1)S(1)}, bf16[4096,512]{1,0:T(8,128)(2,1)}, u32[]{:S(2)}) copy-start(bf16[4096,512]{1,0:T(8,128)(2,1)} %param.11) | copy-start | bytes 12582916
  274.8 41.7 %all-to-all-start.1 = ((bf16[16,40,512]{2,1,0:T(8,128)(2,1)}), bf16[16,40,512]{2,1,0:T(8,128)(2,1)S(1)}, u32[]{:S(2)}, u32[]{:S(2)}) async-start(bf16[16,40,512]{2,1,0:T(8,128)(2,1)} %bitcast.70), calls=%async_computation.2 | async-start | bytes 1310720 | tf_op jit(solution)/shard_map/all_to_all | solution.py:66
  282.2 42.3 %copy-start = (bf16[128,512]{1,0:T(8,128)(2,1)S(1)}, bf16[128,512]{1,0:T(8,128)(2,1)}, u32[]{:S(2)}) copy-start(bf16[128,512]{1,0:T(8,128)(2,1)} %param.13) | copy-start | bytes 393220
  316.5 17.6 %all-to-all-start.3 = ((bf16[16,40,512]{2,1,0:T(8,128)(2,1)}), bf16[16,40,512]{2,1,0:T(8,128)(2,1)S(1)}, u32[]{:S(2)}, u32[]{:S(2)}) async-start(bf16[16,40,512]{2,1,0:T(8,128)(2,1)} %bitcast.69), calls=%async_computation.5 | async-start | bytes 1310720 | tf_op jit(solution)/shard_map/all_to_all | solution.py:66
Sparse Core Ops, SparseCore 0:
  9.7 25.7 all-gather.3
  50.7 23.0 all-gather.5
  223.1 51.6 reduce-scatter.2
  277.0 39.3 reduce-scatter.4
